TPU v7x, 256 devices: a whole 4x4x8 slice. The times are simulated.
256 devices in a mesh: member: 128 (over y, z_lo, x, core), mp: 2 (over z_hi).
Axes of the slice: x: 4, y: 4, z: 8 (z_hi: 2, z_lo: 4; z = z_hi * 4 + z_lo), core: 2. Of those that a mesh axis runs over, the one named last changes fastest.
Arguments:
- token_ids: int32 [512, 64], P('member'), may hold values from 0 to 76031
- fit_ranks: int32 [512], P('member'), may hold values from 0 to 511, as said below
- embed_table: bfloat16 [3584, 76032], P('member'), may hold values from -40 to 40
- norm_gain: float32 [3584], replicated, may hold values from 0.1 to 1.9
- qkv_weight: bfloat16 [3584, 2304], P('member', 'mp'), may hold values from -0.09375 to 0.09375
- qkv_bias: float32 [2304], P('mp'), may hold values from -3 to 3
- out_weight: bfloat16 [3584, 1792], P('member', 'mp'), may hold values from -0.125 to 0.125
- value_weight: float32 [3584], replicated, may hold values from -0.09375 to 0.09375
- qkv_left: bfloat16 [512, 3584], P('member'), may hold values from -5 to 5
- qkv_right: bfloat16 [512, 2304], P('member', 'mp'), may hold values from -5 to 5
- out_left: bfloat16 [512, 1792], P('member', 'mp'), may hold values from -5 to 5
- out_right: bfloat16 [512, 3584], P('member'), may hold values from -5 to 5
Outputs:
- values: float32 [512, 64], P(('member', 'mp'))
- qkv_grad: float32 [3584, 2304], P('member', 'mp')
- out_grad: float32 [3584, 1792], P('member', 'mp')
Inputs may be any that keep to these rules, and one draw needn't show every extreme that they name: `fit_ranks`: A member's rank is the number of members whose integer fitness score is strictly lower; equal scores share a rank.
All inputs are finite; a program needn't handle non-finite values.
Results may differ from a plain program's by a relative error of at most 0.0052.
Values may be sent and summed in bfloat16 or wider, within the bound.
No kernel may reach another device: no remote copies, remote signals or barrier semaphores. Data moves between devices by JAX's collectives and lax.ppermute only.
A program may use at most 128 MiB of HBM per device.

v0:
```python
import math
import jax
import jax.numpy as jnp
from jax import lax
from jax.sharding import PartitionSpec as P

HD = 128
HQ = 14
HK = 2
SIGMA = 0.01
EPSILON = 1e-06
THETA = 1000000.0
MASKED = -1e30


def rope_tables(length, head_size):
    halfway = head_size // 2
    inverse = THETA ** (-(jnp.arange(halfway, dtype=jnp.float32) * 2.0 / head_size))
    places = jnp.arange(length, dtype=jnp.float32)
    angles = places[:, None] * inverse[None, :]
    angles = jnp.concatenate([angles, angles], axis=1)
    return (jnp.cos(angles), jnp.sin(angles))


def rotate(states, cosine, sine_table):
    halfway = states.shape[-1] // 2
    turned = jnp.concatenate([-states[..., halfway:], states[..., :halfway]], axis=-1)
    return states * cosine[None, :, None, :] + turned * sine_table[None, :, None, :]


def attend(query_heads, key_heads, value_heads, kv_count):
    members, length, head_count, head_size = query_heads.shape
    group_size = head_count // kv_count
    grouped = query_heads.reshape(members, length, kv_count, group_size, head_size)
    scores = jnp.einsum(
        "mskgd,mtkd->mkgst", grouped, key_heads, preferred_element_type=jnp.float32
    ) / math.sqrt(head_size)
    causal = jnp.arange(length)[None, :] <= jnp.arange(length)[:, None]
    scores = jnp.where(causal, scores, MASKED)
    top = jnp.max(scores, axis=-1, keepdims=True)
    weights = jnp.exp(scores - top)
    weights = (weights / jnp.sum(weights, axis=-1, keepdims=True)).astype(jnp.bfloat16)
    context = jnp.einsum(
        "mkgst,mtkd->mskgd", weights, value_heads, preferred_element_type=jnp.float32
    )
    return context.astype(jnp.bfloat16).reshape(members, length, head_count * head_size)


def on_device(
    token_ids,
    fit_ranks,
    embed_table,
    norm_gain,
    qkv_weight,
    qkv_bias,
    out_weight,
    value_weight,
    qkv_left,
    qkv_right,
    out_left,
    out_right,
):
    members, length = token_ids.shape
    row_count = members * length
    mp_size = lax.axis_size("mp")
    heads_here = HQ // mp_size
    kv_here = HK // mp_size
    population = members * lax.axis_size("member")
    contract_rows = (((0,), (0,)), ((), ()))
    contract_cols = (((1,), (1,)), ((), ()))
    all_ids = lax.all_gather(token_ids, "member", axis=0, tiled=True)
    picked = jnp.take(embed_table, all_ids.reshape(-1), axis=1)
    embedded = lax.all_to_all(picked, "member", split_axis=1, concat_axis=0, tiled=True)
    features = embedded.astype(jnp.float32)
    inverse_rms = lax.rsqrt(jnp.mean(features * features, axis=0, keepdims=True) + EPSILON)
    normed = (features * inverse_rms * norm_gain[:, None]).astype(jnp.bfloat16)
    base_proj = lax.dot_general(
        normed,
        lax.all_gather(qkv_weight, "member", axis=0, tiled=True),
        contract_rows,
        preferred_element_type=jnp.float32,
    )
    normed_members = normed.reshape(normed.shape[0], members, length)
    coef_in = jnp.einsum("dms,md->ms", normed_members, qkv_left, preferred_element_type=jnp.float32)
    projected = (
        base_proj.reshape(members, length, -1)
        + SIGMA * coef_in[:, :, None] * qkv_right.astype(jnp.float32)[:, None, :]
        + qkv_bias[None, None, :]
    )
    query_width = heads_here * HD
    kv_width = kv_here * HD
    cosine, sine_table = rope_tables(length, HD)
    query_heads = rotate(
        projected[:, :, :query_width].reshape(members, length, heads_here, HD), cosine, sine_table
    ).astype(jnp.bfloat16)
    key_heads = rotate(
        projected[:, :, query_width : query_width + kv_width].reshape(members, length, kv_here, HD),
        cosine,
        sine_table,
    ).astype(jnp.bfloat16)
    value_heads = (
        projected[:, :, query_width + kv_width :]
        .reshape(members, length, kv_here, HD)
        .astype(jnp.bfloat16)
    )
    context = attend(query_heads, key_heads, value_heads, kv_here)
    coef_out = jnp.einsum("msq,mq->ms", context, out_left, preferred_element_type=jnp.float32)
    flat_context = context.reshape(row_count, query_width)
    share_rows = row_count // mp_size
    partial_out = lax.dot_general(
        flat_context,
        lax.all_gather(out_weight, "member", axis=0, tiled=True),
        contract_cols,
        preferred_element_type=jnp.float32,
    )
    head_term = (
        partial_out.reshape(members, length, -1)
        + SIGMA * coef_out[:, :, None] * out_right.astype(jnp.float32)[:, None, :]
    )
    summed = lax.psum_scatter(
        head_term.reshape(row_count, -1), "mp", scatter_dimension=0, tiled=True
    )
    mp_index = lax.axis_index("mp")
    own_embed = lax.dynamic_slice_in_dim(embedded, mp_index * share_rows, share_rows, 1)
    residual = own_embed.T.astype(jnp.float32) + summed
    inverse_out = lax.rsqrt(jnp.mean(residual * residual, axis=1, keepdims=True) + EPSILON)
    value_rows = jnp.sum(residual * inverse_out * value_weight[None, :], axis=1).reshape(
        members // mp_size, length
    )
    rank_values = fit_ranks.astype(jnp.float32)
    first_sum, second_sum = lax.psum(
        (jnp.sum(rank_values), jnp.sum(rank_values * rank_values)), "member"
    )
    center = first_sum / population
    spread = second_sum / population - center * center
    fit_local = (rank_values - center) * lax.rsqrt(spread + EPSILON)
    fitness = lax.all_gather(fit_local, "member", axis=0, tiled=True)
    left_rows, right_rows = (
        lax.all_to_all(qkv_left, "member", split_axis=1, concat_axis=0, tiled=True),
        lax.all_to_all(out_right, "member", split_axis=1, concat_axis=0, tiled=True),
    )
    right_cols, left_cols = (
        lax.all_gather(qkv_right, "member", axis=0, tiled=True),
        lax.all_gather(out_left, "member", axis=0, tiled=True),
    )
    weighted_in = left_rows.astype(jnp.float32) * fitness[:, None]
    qkv_grad = lax.dot_general(
        weighted_in,
        right_cols.astype(jnp.float32),
        contract_rows,
        precision=lax.Precision.HIGHEST,
        preferred_element_type=jnp.float32,
    ) / (population * SIGMA)
    weighted_out = right_rows.astype(jnp.float32) * fitness[:, None]
    out_grad = lax.dot_general(
        weighted_out,
        left_cols.astype(jnp.float32),
        contract_rows,
        precision=lax.Precision.HIGHEST,
        preferred_element_type=jnp.float32,
    ) / (population * SIGMA)
    return (value_rows, qkv_grad, out_grad)


def solution(mesh):
    placed = (
        P("member", None),
        P("member"),
        P("member", None),
        P(),
        P("member", "mp"),
        P("mp"),
        P("member", "mp"),
        P(),
        P("member", None),
        P("member", "mp"),
        P("member", "mp"),
        P("member", None),
    )
    return jax.shard_map(
        on_device,
        mesh=mesh,
        in_specs=placed,
        out_specs=(P(("member", "mp"), None), P("member", "mp"), P("member", "mp")),
        check_vma=False,
    )
```

profile of v0, /device:TPU:128, one launch (start us, length us, event | category | flops | bytes accessed | tf_op | source)
XLA Modules:
  0.0 1395.1 jit_solution(669175354803693460)
XLA Ops:
  7.2 0.7 all-gather.11.cloned.1.call-update
  7.9 0.7 all-gather.9.cloned.1.call-update
  8.6 187.3 %all-gather = s32[128,4,64]{2,1,0:T(4,128)S(1)} all-gather(s32[1,4,64]{2,1,0:T(4,128)} %bitcast.92), channel_id=1, replica_groups=mesh['member'=128,'mp'=2] {'member'}, dimensions={0}, use_global_device_ids=true | all-gather | bytes 132096 | tf_op jit(solution)/shard_map/all_gather | solution.py:71
  196.3 15.8 %copy.45 = bf16[28,76032]{0,1:T(8,128)(2,1)} copy(bf16[28,76032]{1,0:T(8,128)(2,1)} %param.14) | data formatting | bytes 8515584 | tf_op args[2]
  212.2 118.4 %gather_fusion = bf16[32768,28]{1,0:T(8,128)(2,1)} fusion(bf16[28,76032]{0,1:T(8,128)(2,1)} %copy.45, s32[32768]{0:T(1024)S(1)} %broadcast_clamp_fusion), kind=kCustom, calls=%fused_computation | custom fusion | bytes 3801088 | tf_op jit(solution)/shard_map/jit(_take)/gather | solution.py:72
  330.6 7.6 copy.46
  338.4 1.6 broadcast_select_fusion
  340.0 6.3 all-to-all-start
  346.4 0.7 all-gather.13.cloned.1.call-update
  348.0 50.6 %all-to-all-done = bf16[28,128,256]{2,0,1:T(8,128)(2,1)S(1)} async-done(((bf16[28,128,256]{2,0,1:T(8,128)(2,1)}), bf16[28,128,256]{2,0,1:T(8,128)(2,1)S(1)}, u32[]{:S(2)}, u32[]{:S(2)}) %all-to-all-start) | async-done | bytes 1835040 | tf_op jit(solution)/shard_map/all_to_all | solution.py:73
  398.6 1.5 all_to_all.34
  400.8 3.7 fusion.3
  404.5 3.9 copy.47
  408.4 2.4 bitcast_convert_fusion
  410.9 7.8 reshape.204
  418.7 11.5 multiply_convert_fusion
  430.8 10.4 reshape.237
  441.2 12.7 reshape.232
  453.9 5.9 fusion.2
  463.2 6.8 convolution_add_fusion
  469.9 5.1 copy.51
  475.4 0.8 copy.53
  476.2 13.0 all-to-all-start.2
  489.2 199.0 %all-gather.4 = bf16[128,4,896]{2,1,0:T(4,128)(2,1)S(1)} all-gather(bf16[1,4,896]{2,1,0:T(4,128)(2,1)S(1)} %bitcast.91), channel_id=1, replica_groups=mesh['member'=128,'mp'=2] {'member'}, dimensions={0}, use_global_device_ids=true | all-gather | bytes 924672 | tf_op jit(solution)/shard_map/all_gather | solution.py:144
  688.8 338.7 %all-reduce.1 = (f32[]{:T(128)}, f32[]{:T(128)}) all-reduce(f32[]{:T(128)} %get-tuple-element.4, f32[]{:T(128)} %get-tuple-element.3), channel_id=1, replica_groups=mesh['member'=128,'mp'=2] {'member'}, use_global_device_ids=true, to_apply=%region_9.10 | all-reduce | flops 2 | bytes 16 | tf_op jit(solution)/shard_map/psum | solution.py:131
  1030.5 0.8 copy.52
  1032.5 6.2 all-to-all-start.1
  1039.0 340.7 %all-reduce = f32[512]{0:T(512)S(1)} all-reduce(f32[512]{0:T(512)S(1)} %multiply_dynamic-update-slice_fusion), channel_id=1, replica_groups=mesh['member'=128,'mp'=2] {'member'}, use_global_device_ids=true, to_apply=%add | all-reduce | flops 512 | bytes 4096
  1379.9 1.3 convolution_multiply_fusion.2
  1381.2 2.5 reshape.225
  1383.7 1.5 convolution_multiply_fusion
  1385.2 2.1 multiply_reduce_fusion.2
  (79 shorter events, 9.7 us)
Async XLA Ops:
  7.2 423.6 %all-gather.11.cloned.1.call-start = ((), (), s32[]{:S(2)}) async-start(), calls=%async_computation.6 | async-start | bytes 7397376 | tf_op jit(solution)/shard_map/all_gather | solution.py:112
  7.9 433.3 %all-gather.9.cloned.1.call-start = ((), (), s32[]{:S(2)}) async-start(), calls=%async_computation.5 | async-start | bytes 9510912 | tf_op jit(solution)/shard_map/all_gather | solution.py:79
  340.0 7.1 copy-start.6
  340.0 7.2 copy-start.3
  340.0 58.6 %all-to-all-start = ((bf16[28,128,256]{2,0,1:T(8,128)(2,1)}), bf16[28,128,256]{2,0,1:T(8,128)(2,1)S(1)}, u32[]{:S(2)}, u32[]{:S(2)}) async-start(bf16[28,128,256]{2,0,1:T(8,128)(2,1)} %broadcast_select_fusion), calls=%async_computation | async-start | bytes 4194304 | tf_op jit(solution)/shard_map/all_to_all | solution.py:73
  346.3 1034.9 %all-gather.13.cloned.1.call-start = ((), (), s32[]{:S(2)}) async-start(), calls=%async_computation.7 | async-start | bytes 1188864 | tf_op jit(solution)/shard_map/all_gather | solution.py:143
  347.1 1038.1 %reduce-scatter.2.cloned.1.call-start = ((), (), s32[]{:S(2)}) async-start(), calls=%async_computation.4 | async-start | bytes 5505024 | tf_op jit(solution)/shard_map/reduce_scatter | solution.py:120
  398.6 2.2 copy-start.4
  418.6 11.5 copy-start.7
  441.2 12.7 copy-start.2
  441.2 12.7 copy-start.11
  461.7 1.2 copy-start.9
  462.0 1.1 copy-start.5
  475.1 213.2 %copy-start.10 = (s32[4]{0:T(128)S(1)}, s32[4]{0:T(128)}, u32[]{:S(2)}) copy-start(s32[4]{0:T(128)} %param.13) | copy-start | bytes 52
  475.1 556.2 %copy-start.12 = (u32[256]{0:T(256)S(1)}, u32[256]{0:T(256)}, u32[]{:S(2)}) copy-start(u32[256]{0:T(256)} %constant.74) | copy-start | bytes 3076
  476.2 556.4 %all-to-all-start.2 = ((bf16[4,128,28]{2,0,1:T(4,128)(2,1)}), bf16[4,128,28]{2,0,1:T(4,128)(2,1)S(1)}, u32[]{:S(2)}, u32[]{:S(2)}) async-start(bf16[4,128,28]{2,0,1:T(4,128)(2,1)} %copy.53), calls=%async_computation.3 | async-start | bytes 262144 | tf_op jit(solution)/shard_map/all_to_all | solution.py:140
  1032.5 347.3 %all-to-all-start.1 = ((bf16[4,128,28]{2,0,1:T(4,128)(2,1)}), bf16[4,128,28]{2,0,1:T(4,128)(2,1)S(1)}, u32[]{:S(2)}, u32[]{:S(2)}) async-start(bf16[4,128,28]{2,0,1:T(4,128)(2,1)} %copy.52), calls=%async_computation.2 | async-start | bytes 262144 | tf_op jit(solution)/shard_map/all_to_all | solution.py:139
  1381.2 4.0 copy-start
  1383.7 3.6 copy-start.8
  1385.2 2.1 copy-start.1
Sparse Core Ops, SparseCore 0:
  9.8 203.6 all-gather.10
  215.4 217.5 all-gather.8
  434.9 196.6 all-gather.12
  634.0 90.6 reduce-scatter.1
where the time goes:
time: 1400 us
  blocking collectives  1070 us (76%)
  local copies, waits for them, and re-layouts  191 us (14%)
  waiting for transfers between devices  52.6 us (4%)
  starting transfers between devices  25.7 us (2%)
  other arithmetic  25.4 us (2%)
  between operations  17.4 us (1%)
  matrix products  17.2 us (1%)
    unnamed x1, blocking collectives  341 us
    psum x1, blocking collectives, on_device(): lax.psum((jnp.sum(rank_values), jnp.sum(rank_values * rank_values)), 'mem...  339 us
    all_gather x1, blocking collectives, on_device(): lax.all_gather(out_left, 'member', axis=0, tiled=True)  199 us
    all_gather x1, blocking collectives, on_device(): all_ids = lax.all_gather(token_ids, 'member', axis=0, tiled=True)  187 us
    gather x2, local copies, waits for them, and re-layouts, on_device(): picked = jnp.take(embed_table, all_ids.reshape(-1), axis=1)  126 us
    all_to_all x1, waiting for transfers between devices, on_device(): lax.all_to_all(picked, 'member', split_axis=1, concat_axis=0, tiled=True)  50.6 us
    unnamed x33, local copies, waits for them, and re-layouts  42.2 us
  transfers between devices with their start and end apart: 7, of which 1 were waited for; matrix products, arithmetic and copies ran while one was open for 16% of the time, Pallas kernels for 0%

commit v1 on v0

--- a/solution.py
+++ b/solution.py
@@ -139,9 +139,15 @@
         lax.all_to_all(qkv_left, "member", split_axis=1, concat_axis=0, tiled=True),
         lax.all_to_all(out_right, "member", split_axis=1, concat_axis=0, tiled=True),
     )
+
+    def tell_the_unit(load, device_axis):
+        v_now = jnp.stack([load] * lax.axis_size(device_axis), axis=0)
+        met_up = lax.all_to_all(v_now, axis_name=device_axis, split_axis=0, concat_axis=0)
+        return jnp.concatenate(met_up, axis=0)
+
     right_cols, left_cols = (
         lax.all_gather(qkv_right, "member", axis=0, tiled=True),
-        lax.all_gather(out_left, "member", axis=0, tiled=True),
+        tell_the_unit(out_left, "member"),
     )
     weighted_in = left_rows.astype(jnp.float32) * fitness[:, None]
     qkv_grad = lax.dot_general(

time: 1400 us -> 1240 us (0.89)
  blocking collectives: 1070 us -> 895 us
    all_gather x1 -> x0, blocking collectives: 199 us -> none  [on_device(): lax.all_gather(out_left, 'member', axis=0, tiled=True)]
    psum x1, blocking collectives: 339 us -> 358 us  [on_device(): lax.psum((jnp.sum(rank_values), jnp.sum(rank_values * rank_values)), 'mem...]
    all_to_all x0 -> x1, blocking collectives: none -> 16.4 us  [on_device(): lax.all_to_all(out_right, 'member', split_axis=1, concat_axis=0, tiled=True)]
    unnamed x33 -> x32, local copies, waits for them, and re-layouts: 42.2 us -> 42 us
  transfers between devices with their start and end apart: 7 -> 7, of which waited for: 1 -> 2; matrix products, arithmetic and copies ran while one was open for 16% -> 19% of each run, Pallas kernels for 0% -> 0%
where the time goes in v1:
time: 1240 us; the launch traced here: 1230 us
  blocking collectives  895 us (72%)
  local copies, waits for them, and re-layouts  191 us (15%)
  waiting for transfers between devices  62.8 us (5%)
  starting transfers between devices  25.7 us (2%)
  other arithmetic  25.6 us (2%)
  between operations  17.4 us (1%)
  matrix products  17.1 us (1%)
    psum x1, blocking collectives, on_device(): lax.psum((jnp.sum(rank_values), jnp.sum(rank_values * rank_values)), 'mem...  358 us
    unnamed x1, blocking collectives  333 us
    all_gather x1, blocking collectives, on_device(): all_ids = lax.all_gather(token_ids, 'member', axis=0, tiled=True)  187 us
    gather x2, local copies, waits for them, and re-layouts, on_device(): picked = jnp.take(embed_table, all_ids.reshape(-1), axis=1)  126 us
    all_to_all x1, waiting for transfers between devices, on_device(): lax.all_to_all(picked, 'member', split_axis=1, concat_axis=0, tiled=True)  50.6 us
    unnamed x32, local copies, waits for them, and re-layouts  42 us
  transfers between devices with their start and end apart: 7, of which 2 were waited for; matrix products, arithmetic and copies ran while one was open for 19% of the time, Pallas kernels for 0%

profile of v1, /device:TPU:128, one launch (start us, length us, event | category | flops | bytes accessed | tf_op | source)
XLA Modules:
  0.0 1234.9 jit_solution(1875016032741504963)
XLA Ops:
  7.2 0.7 all-gather.10.cloned.1.call-update
  7.9 0.7 all-gather.8.cloned.1.call-update
  8.6 187.3 %all-gather = s32[128,4,64]{2,1,0:T(4,128)S(1)} all-gather(s32[1,4,64]{2,1,0:T(4,128)} %bitcast.91), channel_id=1, replica_groups=mesh['member'=128,'mp'=2] {'member'}, dimensions={0}, use_global_device_ids=true | all-gather | bytes 132096 | tf_op jit(solution)/shard_map/all_gather | solution.py:71
  196.3 15.8 %copy.48 = bf16[28,76032]{0,1:T(8,128)(2,1)} copy(bf16[28,76032]{1,0:T(8,128)(2,1)} %param.14) | data formatting | bytes 8515584 | tf_op args[2]
  212.2 118.4 %gather_fusion = bf16[32768,28]{1,0:T(8,128)(2,1)} fusion(bf16[28,76032]{0,1:T(8,128)(2,1)} %copy.48, s32[32768]{0:T(1024)S(1)} %broadcast_clamp_fusion), kind=kCustom, calls=%fused_computation | custom fusion | bytes 3801088 | tf_op jit(solution)/shard_map/jit(_take)/gather | solution.py:72
  330.6 7.6 copy.49
  338.4 1.6 broadcast_select_fusion
  340.0 6.3 all-to-all-start
  348.0 50.6 %all-to-all-done = bf16[28,128,256]{2,0,1:T(8,128)(2,1)S(1)} async-done(((bf16[28,128,256]{2,0,1:T(8,128)(2,1)}), bf16[28,128,256]{2,0,1:T(8,128)(2,1)S(1)}, u32[]{:S(2)}, u32[]{:S(2)}) %all-to-all-start) | async-done | bytes 1835040 | tf_op jit(solution)/shard_map/all_to_all | solution.py:73
  398.6 1.5 all_to_all.37
  400.8 3.7 fusion.3
  404.5 3.9 copy.50
  408.4 2.4 bitcast_convert_fusion
  410.9 7.8 reshape.210
  418.7 11.5 multiply_convert_fusion
  430.8 10.4 reshape.240
  441.2 12.7 %reshape.235 = bf16[3584,1152,1]{1,0,2:T(8,128)(2,1)} reshape(bf16[128,28,1152]{2,1,0:T(8,128)(2,1)} %all-gather.8.cloned.1.call-done) | data formatting | bytes 16515072
  453.9 5.9 fusion.2
  463.2 6.8 convolution_add_fusion
  469.9 5.1 copy.54
  475.4 0.8 copy.55
  476.2 13.0 %all-to-all-start.1 = ((bf16[4,128,28]{2,0,1:T(4,128)(2,1)}), bf16[4,128,28]{2,0,1:T(4,128)(2,1)S(1)}, u32[]{:S(2)}, u32[]{:S(2)}) async-start(bf16[4,128,28]{2,0,1:T(4,128)(2,1)} %copy.55), calls=%async_computation.2 | async-start | bytes 262144 | tf_op jit(solution)/shard_map/all_to_all | solution.py:139
  489.7 10.1 all-to-all-done.1
  499.8 16.4 %all_to_all.47 = bf16[4,128,28]{2,0,1:T(4,128)(2,1)S(1)} all-to-all(bf16[4,128,28]{2,0,1:T(4,128)(2,1)S(1)} %copy.56), channel_id=1, replica_groups=mesh['member'=128,'mp'=2] {'member'}, dimensions={1} | all-to-all | bytes 57344 | tf_op jit(solution)/shard_map/all_to_all | solution.py:140
  516.2 1.2 stack.2
  517.4 6.2 all-to-all-start.3
  524.2 357.8 %all-reduce.1 = (f32[]{:T(128)}, f32[]{:T(128)}) all-reduce(f32[]{:T(128)} %get-tuple-element.4, f32[]{:T(128)} %get-tuple-element.3), channel_id=1, replica_groups=mesh['member'=128,'mp'=2] {'member'}, use_global_device_ids=true, to_apply=%region_9.10 | all-reduce | flops 2 | bytes 16 | tf_op jit(solution)/shard_map/psum | solution.py:131
  886.0 333.4 %all-reduce = f32[512]{0:T(512)S(1)} all-reduce(f32[512]{0:T(512)S(1)} %multiply_dynamic-update-slice_fusion), channel_id=1, replica_groups=mesh['member'=128,'mp'=2] {'member'}, use_global_device_ids=true, to_apply=%add | all-reduce | flops 512 | bytes 4096
  1219.8 1.2 fusion.7
  1221.0 2.5 reshape.230
  1223.5 1.5 convolution_multiply_fusion
  1225.0 2.1 multiply_reduce_fusion.2
  (80 shorter events, 10.6 us)
Async XLA Ops:
  7.2 423.6 %all-gather.10.cloned.1.call-start = ((), (), s32[]{:S(2)}) async-start(), calls=%async_computation.7 | async-start | bytes 7397376 | tf_op jit(solution)/shard_map/all_gather | solution.py:112
  7.9 433.3 %all-gather.8.cloned.1.call-start = ((), (), s32[]{:S(2)}) async-start(), calls=%async_computation.6 | async-start | bytes 9510912 | tf_op jit(solution)/shard_map/all_gather | solution.py:79
  340.0 7.1 copy-start.6
  340.0 7.2 copy-start.3
  340.0 58.6 %all-to-all-start = ((bf16[28,128,256]{2,0,1:T(8,128)(2,1)}), bf16[28,128,256]{2,0,1:T(8,128)(2,1)S(1)}, u32[]{:S(2)}, u32[]{:S(2)}) async-start(bf16[28,128,256]{2,0,1:T(8,128)(2,1)} %broadcast_select_fusion), calls=%async_computation | async-start | bytes 4194304 | tf_op jit(solution)/shard_map/all_to_all | solution.py:73
  346.3 874.6 %all-gather.12.cloned.1.call-start = ((), (), s32[]{:S(2)}) async-start(), calls=%async_computation.8 | async-start | bytes 1188864 | tf_op jit(solution)/shard_map/all_gather | solution.py:149
  347.1 877.9 %reduce-scatter.2.cloned.1.call-start = ((), (), s32[]{:S(2)}) async-start(), calls=%async_computation.5 | async-start | bytes 5505024 | tf_op jit(solution)/shard_map/reduce_scatter | solution.py:120
  398.6 2.2 copy-start.4
  418.6 11.5 copy-start.7
  441.2 12.7 %copy-start.2 = (bf16[256,3584]{1,0:T(8,128)(2,1)S(1)}, bf16[256,3584]{1,0:T(8,128)(2,1)}, u32[]{:S(2)}) copy-start(bf16[256,3584]{1,0:T(8,128)(2,1)} %copy.50) | copy-start | bytes 5505028
  441.2 12.7 %copy-start.11 = (f32[1152]{0:T(1024)S(1)}, f32[1152]{0:T(1024)}, u32[]{:S(2)}) copy-start(f32[1152]{0:T(1024)} %param.17) | copy-start | bytes 13828
  461.7 1.2 copy-start.9
  462.0 1.1 copy-start.5
  475.1 48.5 %copy-start.10 = (s32[4]{0:T(128)S(1)}, s32[4]{0:T(128)}, u32[]{:S(2)}) copy-start(s32[4]{0:T(128)} %param.13) | copy-start | bytes 52
  475.1 409.5 %copy-start.12 = (u32[256]{0:T(256)S(1)}, u32[256]{0:T(256)}, u32[]{:S(2)}) copy-start(u32[256]{0:T(256)} %constant.74) | copy-start | bytes 3076
  476.2 23.6 %all-to-all-start.1 = ((bf16[4,128,28]{2,0,1:T(4,128)(2,1)}), bf16[4,128,28]{2,0,1:T(4,128)(2,1)S(1)}, u32[]{:S(2)}, u32[]{:S(2)}) async-start(bf16[4,128,28]{2,0,1:T(4,128)(2,1)} %copy.55), calls=%async_computation.2 | async-start | bytes 262144 | tf_op jit(solution)/shard_map/all_to_all | solution.py:139
  517.4 702.4 %all-to-all-start.3 = ((bf16[128,4,896]{2,1,0:T(4,128)(2,1)}), bf16[128,4,896]{2,1,0:T(4,128)(2,1)S(1)}, u32[]{:S(2)}, u32[]{:S(2)}) async-start(bf16[128,4,896]{2,1,0:T(4,128)(2,1)} %stack.2), calls=%async_computation.4 | async-start | bytes 1835008 | tf_op jit(solution)/shard_map/all_to_all | solution.py:145
  1221.0 4.0 copy-start
  1223.5 3.6 copy-start.8
  1225.0 2.1 copy-start.1
Sparse Core Ops, SparseCore 0:
  9.8 203.6 all-gather.9
  215.4 217.5 all-gather.7
  434.9 198.6 all-gather.11
  635.9 90.8 reduce-scatter.1
